TPU v7x, 128 devices: a whole 4x4x4 slice. The times are simulated.
128 devices in a mesh: section: 4 (over x), sample: 8 (over z, y_lo), tensor: 4 (over y_hi, core).
Axes of the slice: x: 4, y: 4 (y_hi: 2, y_lo: 2; y = y_hi * 2 + y_lo), z: 4, core: 2. Of those that a mesh axis runs over, the one named last changes fastest.
Arguments:
- queries: bfloat16 [4, 1024, 8192], P('section', 'sample', 'tensor'), may hold values from -4.5 to 4.5
- suffix_keys: bfloat16 [4, 1024, 1024], P('section', 'sample', 'tensor'), may hold values from -4.5 to 4.5
- suffix_values: bfloat16 [4, 1024, 1024], P('section', 'sample', 'tensor'), may hold values from -4.5 to 4.5
- output_grad: bfloat16 [4, 1024, 8192], P('section', 'sample', 'tensor'), may hold values from -192 to 192
- prefix_keys: bfloat16 [4, 4096, 1024], P('section', ('sample', 'tensor')), may hold values from -4.5 to 4.5
- prefix_values: bfloat16 [4, 4096, 1024], P('section', ('sample', 'tensor')), may hold values from -4.5 to 4.5
- kv_weight: bfloat16 [4, 8192, 2, 1024], P('section', None, None, 'tensor'), may hold values from -0.0625 to 0.0625
- prefix_states: bfloat16 [4, 4096, 8192], P('section', ('sample', 'tensor')), may hold values from -6 to 6
- norm_gain: bfloat16 [4, 8192], P('section'), may hold values from 0.099609375 to 1.8984375
- segment_ids: int32 [8, 128], P('sample'), may hold values from 0 to 1, never falling along the last dimension, each value on 1 to 96 neighbouring positions
- segment_prompt: int32 [8, 2], P('sample'), may hold values from 0 to 2
- block_table: int32 [3, 16], replicated, may hold values from 0 to 31, as said below
Outputs:
- query_grad: bfloat16 [4, 1024, 8192], P('section', 'sample', 'tensor')
- rollout_key_gradient: bfloat16 [4, 1024, 1024], P('section', 'sample', 'tensor')
- suffix_value_grad: bfloat16 [4, 1024, 1024], P('section', 'sample', 'tensor')
- prefix_key_grad: float32 [4, 4096, 1024], P('section', ('sample', 'tensor'))
- prefix_value_grad: float32 [4, 4096, 1024], P('section', ('sample', 'tensor'))
- prefix_state_gradient: float32 [4, 4096, 8192], P('section', ('sample', 'tensor'))
Inputs may be any that keep to these rules, and one draw needn't show every extreme that they name: `block_table`: each row lists 16 distinct pages; its first 8 entries are the same pages in every row, and every page of the pool appears in some row.
All inputs are finite; a program needn't handle non-finite values.
Results may differ from a plain program's by a relative error of at most 0.024.
Values may be sent and summed in bfloat16 or wider, within the bound.
No kernel may reach another device: no remote copies, remote signals or barrier semaphores. Data moves between devices by JAX's collectives and lax.ppermute only.
A program may use at most 192 MiB of HBM per device.

v0:
```python
import jax
import jax.numpy as jnp
from jax import lax
from jax.sharding import PartitionSpec as P

HEAD_SIZE = 128
PAGE = 128
MASKED_SCORE = -1e30
EPSILON = 1e-05


def visible_keys(seg_row, prompt_row, table, pooled_rows):
    tok_count = seg_row.shape[0]
    seg_hot = seg_row[:, None] == jnp.arange(prompt_row.shape[0], dtype=jnp.int32)[None, :]
    prompt_tok = jnp.sum(jnp.where(seg_hot, prompt_row[None, :], 0), axis=1)
    page_ids = jnp.arange(pooled_rows // PAGE, dtype=jnp.int32)
    member = jnp.any(table[:, :, None] == page_ids[None, None, :], axis=1)
    prompt_hot = prompt_tok[:, None] == jnp.arange(table.shape[0], dtype=jnp.int32)[None, :]
    member_tok = jnp.any(prompt_hot[:, :, None] & member[None, :, :], axis=1)
    prefix_seen = jnp.repeat(member_tok, PAGE, axis=1)
    position = jnp.arange(tok_count, dtype=jnp.int32)
    suffix_seen = (seg_row[:, None] == seg_row[None, :]) & (position[None, :] <= position[:, None])
    return jnp.concatenate([prefix_seen, suffix_seen], axis=1)


def attend_group(query_grp, grad_grp, key_rows, value_rows, visible):
    inv_root = query_grp.shape[-1] ** (-0.5)
    scores = (
        jnp.einsum("rgd,kd->rgk", query_grp, key_rows, preferred_element_type=jnp.float32)
        * inv_root
    )
    scores = jnp.where(visible[:, None, :], scores, MASKED_SCORE)
    row_max = jnp.max(scores, axis=2, keepdims=True)
    exponent = jnp.exp(scores - row_max)
    softmax_w = exponent / jnp.sum(exponent, axis=2, keepdims=True)
    weights_low = softmax_w.astype(jnp.bfloat16)
    attended = jnp.einsum(
        "rgk,kd->rgd", weights_low, value_rows, preferred_element_type=jnp.float32
    )
    delta_row = jnp.sum(grad_grp.astype(jnp.float32) * attended, axis=2, keepdims=True)
    weight_grad = jnp.einsum(
        "rgd,kd->rgk", grad_grp, value_rows, preferred_element_type=jnp.float32
    )
    score_grad = (softmax_w * (weight_grad - delta_row)).astype(jnp.bfloat16)
    query_out = (
        jnp.einsum("rgk,kd->rgd", score_grad, key_rows, preferred_element_type=jnp.float32)
        * inv_root
    )
    key_result = (
        jnp.einsum("rgk,rgd->kd", score_grad, query_grp, preferred_element_type=jnp.float32)
        * inv_root
    )
    value_out = jnp.einsum("rgk,rgd->kd", weights_low, grad_grp, preferred_element_type=jnp.float32)
    return (query_out, key_result, value_out)


def make_body(n_sec, n_smp, n_ten):

    def on_device(
        queries,
        suffix_keys,
        suffix_values,
        output_grad,
        prefix_keys,
        prefix_values,
        kv_weight,
        prefix_states,
        norm_gain,
        segment_ids,
        segment_prompt,
        block_table,
    ):
        head_width = suffix_keys.shape[2]
        kv_local = head_width // HEAD_SIZE
        rows_local = prefix_keys.shape[1]
        pooled_rows = rows_local * n_smp * n_ten
        block_rows = rows_local * n_ten
        tok_count = queries.shape[1]
        group_size = queries.shape[2] // head_width
        visible = visible_keys(segment_ids[0], segment_prompt[0], block_table, pooled_rows)
        query_rows = queries[0].reshape(tok_count, kv_local, group_size, HEAD_SIZE)
        grad_rows = output_grad[0].reshape(tok_count, kv_local, group_size, HEAD_SIZE)
        own_keys = suffix_keys[0]
        own_values = suffix_values[0]
        pk = prefix_keys[0].reshape(rows_local, n_ten, kv_local, HEAD_SIZE)
        pv = prefix_values[0].reshape(rows_local, n_ten, kv_local, HEAD_SIZE)
        query_pieces, suffix_key_pieces, suffix_value_pieces, reduced_pieces = ([], [], [], [])
        for head_index in range(kv_local):
            low_col = head_index * HEAD_SIZE
            send = jnp.concatenate([pk[:, :, head_index], pv[:, :, head_index]], axis=-1)
            send = send.transpose(1, 0, 2)
            got = lax.all_to_all(send, "tensor", 0, 0, tiled=True)
            got = got.reshape(block_rows, 2 * HEAD_SIZE)
            pool = lax.all_gather(got, "sample", axis=0, tiled=True)
            key_rows = jnp.concatenate(
                [pool[:, :HEAD_SIZE], own_keys[:, low_col : low_col + HEAD_SIZE]], axis=0
            )
            value_rows = jnp.concatenate(
                [pool[:, HEAD_SIZE:], own_values[:, low_col : low_col + HEAD_SIZE]], axis=0
            )
            query_out, key_result, value_out = attend_group(
                query_rows[:, head_index], grad_rows[:, head_index], key_rows, value_rows, visible
            )
            query_pieces.append(query_out)
            suffix_key_pieces.append(key_result[pooled_rows:])
            suffix_value_pieces.append(value_out[pooled_rows:])
            pool_grad = jnp.concatenate(
                [key_result[:pooled_rows], value_out[:pooled_rows]], axis=1
            ).astype(jnp.bfloat16)
            reduced_pieces.append(
                lax.psum_scatter(pool_grad, "sample", scatter_dimension=0, tiled=True)
            )
        query_grad = jnp.stack(query_pieces, axis=1).reshape(tok_count, -1).astype(jnp.bfloat16)
        rollout_key_gradient = jnp.concatenate(suffix_key_pieces, axis=1).astype(jnp.bfloat16)
        suffix_value_grad = jnp.concatenate(suffix_value_pieces, axis=1).astype(jnp.bfloat16)
        reduced = jnp.concatenate(reduced_pieces, axis=1)
        home_send = reduced.reshape(n_ten, rows_local, kv_local * 2 * HEAD_SIZE)
        home = lax.all_to_all(home_send, "tensor", 0, 0, tiled=True)
        home = home.reshape(n_ten, rows_local, kv_local, 2, HEAD_SIZE).transpose(3, 1, 0, 2, 4)
        home = home.reshape(2, rows_local, n_ten * kv_local * HEAD_SIZE).astype(jnp.float32)
        key_home = home[0]
        value_home = home[1]
        grad_cols = reduced.reshape(block_rows, kv_local, 2, HEAD_SIZE).transpose(0, 2, 1, 3)
        grad_cols = grad_cols.reshape(block_rows, 2, kv_local * HEAD_SIZE)
        group_term = lax.dot_general(
            grad_cols,
            kv_weight[0],
            (((1, 2), (1, 2)), ((), ())),
            preferred_element_type=jnp.float32,
        ).astype(jnp.bfloat16)
        width = group_term.shape[1]
        t_idx = lax.axis_index("tensor")
        core = t_idx % 2
        hi = t_idx // 2
        term4 = group_term.reshape(2, 2, rows_local, width)
        keep = lax.dynamic_index_in_dim(term4, core, 1, False)
        give = lax.dynamic_index_in_dim(term4, 1 - core, 1, False)
        core_pairs = [(i, i ^ 1) for i in range(n_ten)]
        got1 = lax.ppermute(give, "tensor", core_pairs)
        partial = keep.astype(jnp.float32) + got1.astype(jnp.float32)
        mine = lax.dynamic_index_in_dim(partial, hi, 0, False)
        other = lax.dynamic_index_in_dim(partial, 1 - hi, 0, False)
        chip_pairs = [(i, i ^ 2) for i in range(n_ten)]
        got2 = lax.ppermute(other.astype(jnp.bfloat16), "tensor", chip_pairs)
        normed_grad = mine + got2.astype(jnp.float32)
        states = prefix_states[0].astype(jnp.float32)
        gain_wide = norm_gain[0].astype(jnp.float32)[None, :]
        inv_rms = lax.rsqrt(jnp.mean(states * states, axis=1, keepdims=True) + EPSILON)
        gained = gain_wide * normed_grad
        layer_term = inv_rms * gained - states * inv_rms**3 * jnp.mean(
            states * gained, axis=1, keepdims=True
        )
        term_low = layer_term.astype(jnp.bfloat16)
        prefix_state_gradient = layer_term
        for shift in range(1, n_sec):
            pairs = [(l + shift, l) for l in range(n_sec - shift)]
            prefix_state_gradient = prefix_state_gradient + lax.ppermute(
                term_low, "section", pairs
            ).astype(jnp.float32)
        return (
            query_grad[None],
            rollout_key_gradient[None],
            suffix_value_grad[None],
            key_home[None],
            value_home[None],
            prefix_state_gradient[None],
        )

    return on_device


def solution(mesh):
    placed = (
        P("section", "sample", "tensor"),
        P("section", "sample", "tensor"),
        P("section", "sample", "tensor"),
        P("section", "sample", "tensor"),
        P("section", ("sample", "tensor"), None),
        P("section", ("sample", "tensor"), None),
        P("section", None, None, "tensor"),
        P("section", ("sample", "tensor"), None),
        P("section", None),
        P("sample", None),
        P("sample", None),
        P(),
    )
    body = make_body(mesh.shape["section"], mesh.shape["sample"], mesh.shape["tensor"])
    return jax.shard_map(
        body,
        mesh=mesh,
        in_specs=placed,
        out_specs=(
            P("section", "sample", "tensor"),
            P("section", "sample", "tensor"),
            P("section", "sample", "tensor"),
            P("section", ("sample", "tensor"), None),
            P("section", ("sample", "tensor"), None),
            P("section", ("sample", "tensor"), None),
        ),
        check_vma=False,
    )
```

profile of v0, /device:TPU:3, one launch (start us, length us, event | category | flops | bytes accessed | tf_op | source)
XLA Modules:
  0.0 443.0 jit_solution(18335856734817122372)
XLA Ops:
  10.4 11.5 %all_to_all.15 = bf16[4,128,256]{2,1,0:T(8,128)(2,1)} all-to-all(bf16[4,128,256]{2,1,0:T(8,128)(2,1)S(1)} %maximum_bitcast_fusion.12), channel_id=1, replica_groups=mesh['section'=4,'sample'=8,'tensor'=4] {'tensor'}, dimensions={0} | all-to-all | bytes 524288 | tf_op jit(solution)/shard_map/all_to_all | solution.py:92
  22.8 4.4 all-to-all-start.1
  30.1 1.4 fusion.65
  31.4 2.3 all-to-all-done.1
  34.5 39.4 %all-gather.3.cloned.1.call-done = bf16[4096,256]{1,0:T(8,128)(2,1)} async-done(((bf16[512,256]{1,0:T(8,128)(2,1)}), bf16[4096,256]{1,0:T(8,128)(2,1)}) %all-gather.3.cloned.1.call-update) | async-done | bytes 2097168 | tf_op jit(solution)/shard_map/all_gather | solution.py:94
  73.9 2.6 fusion.59
  77.6 2.4 fusion.34
  80.0 10.7 %fusion.68 = (f32[128,8]{0,1:T(8,128)S(1)}, f32[128,8,4224]{0,2,1:T(8,128)}) fusion(f32[4224,128,8]{1,0,2:T(8,128)S(1)} %fusion.34, pred[128,4224]{0,1:T(8,128)(4,1)S(1)} %pad_add_fusion), kind=kOutput, calls=%fused_computation.127 | output fusion | flops 17305728 | bytes 35147776 | tf_op jit(solution)/shard_map/sub | solution.py:34
  90.8 7.5 %fusion.13 = bf16[128,8,4224]{0,2,1:T(8,128)(2,1)S(1)} fusion(f32[128,8,4224]{0,2,1:T(8,128)} %get-tuple-element.53, f32[128,8]{0,1:T(8,128)S(1)} %get-tuple-element.52), kind=kLoop, calls=%fused_computation.23 | loop fusion | flops 8650752 | bytes 25956352 | tf_op jit(solution)/shard_map/convert_element_type | solution.py:36
  98.4 4.4 copy-done.5
  102.8 2.5 fusion.29
  105.5 6.2 %fusion.3 = bf16[128,8,4224]{0,2,1:T(8,128)(2,1)} fusion(f32[128,8]{0,1:T(8,128)S(1)} %fusion.29, f32[128,8,4224]{0,2,1:T(8,128)S(1)} %bitcast.189, f32[128,8]{0,1:T(8,128)S(1)} %get-tuple-element.52, bf16[128,128]{1,0:T(8,128)(2,1)} %get-tuple-element.44, bf16[4096,128]{1,0:T(8,128)(2,1)} %get-tuple-element.32, bf16[128,2,8,128]{0,3,2,1:T(8,128)(2,1)S(1)} %bitcast.199), kind=kOutput, calls=%fused_computation.6 | convolution fusion | flops 1126760448 | bytes 27303936 | tf_op jit(solution)/shard_map/rgd,kd->rgk/dot_general | solution.py:41
  111.7 6.5 %fusion.17 = bf16[4224,128]{0,1:T(8,128)(2,1)S(1)} fusion(bf16[128,8,4224]{0,2,1:T(8,128)(2,1)} %fusion.3, bf16[128,2,8,128]{0,3,2,1:T(8,128)(2,1)S(1)} %bitcast.194), kind=kOutput, calls=%fused_computation.34 | convolution fusion | flops 1108377600 | bytes 9994240 | tf_op jit(solution)/shard_map/rgk,rgd->kd/dot_general | solution.py:50
  118.3 2.9 fusion.19
  122.2 1.5 pad_maximum_fusion
  123.8 4.6 %all-gather.5.cloned.1.call-done = bf16[4096,256]{1,0:T(8,128)(2,1)} async-done(((bf16[512,256]{1,0:T(8,128)(2,1)}), bf16[4096,256]{1,0:T(8,128)(2,1)}) %all-gather.5.cloned.1.call-update) | async-done | bytes 2097168 | tf_op jit(solution)/shard_map/all_gather | solution.py:94
  128.4 2.6 fusion.60
  132.0 2.4 fusion.33
  134.4 10.4 %fusion.67 = (f32[128,8]{0,1:T(8,128)S(1)}, f32[128,8,4224]{0,2,1:T(8,128)}) fusion(f32[4224,128,8]{1,0,2:T(8,128)S(1)} %fusion.33, pred[128,4224]{0,1:T(8,128)(4,1)S(1)} %pad_add_fusion), kind=kOutput, calls=%fused_computation.126 | output fusion | flops 17305728 | bytes 35147776 | tf_op jit(solution)/shard_map/sub | solution.py:34
  144.8 7.6 %fusion.14 = bf16[128,8,4224]{0,2,1:T(8,128)(2,1)S(1)} fusion(f32[128,8,4224]{0,2,1:T(8,128)} %get-tuple-element.51, f32[128,8]{0,1:T(8,128)S(1)} %get-tuple-element.50), kind=kLoop, calls=%fused_computation.24 | loop fusion | flops 8650752 | bytes 25956352 | tf_op jit(solution)/shard_map/convert_element_type | solution.py:36
  152.4 4.4 copy-done.3
  156.8 2.5 fusion.30
  159.5 6.1 %fusion.2 = bf16[128,8,4224]{0,2,1:T(8,128)(2,1)} fusion(f32[128,8]{0,1:T(8,128)S(1)} %fusion.30, f32[128,8,4224]{0,2,1:T(8,128)S(1)} %bitcast.187, f32[128,8]{0,1:T(8,128)S(1)} %get-tuple-element.50, bf16[128,128]{1,0:T(8,128)(2,1)S(1)} %copy-done.28, bf16[4096,128]{1,0:T(8,128)(2,1)} %get-tuple-element.34, bf16[128,2,8,128]{0,3,2,1:T(8,128)(2,1)S(1)} %bitcast.201), kind=kOutput, calls=%fused_computation.3 | convolution fusion | flops 1126760448 | bytes 27303936 | tf_op jit(solution)/shard_map/rgd,kd->rgk/dot_general | solution.py:41
  165.6 6.5 %fusion.18 = bf16[4224,128]{0,1:T(8,128)(2,1)S(1)} fusion(bf16[128,8,4224]{0,2,1:T(8,128)(2,1)} %fusion.2, bf16[128,2,8,128]{0,3,2,1:T(8,128)(2,1)S(1)} %bitcast.196), kind=kOutput, calls=%fused_computation.35 | convolution fusion | flops 1108377600 | bytes 9994240 | tf_op jit(solution)/shard_map/rgk,rgd->kd/dot_general | solution.py:50
  173.3 2.9 fusion.20
  177.3 1.5 pad_maximum_fusion.1
  178.9 4.7 %reduce-scatter.3.cloned.1.call-done = bf16[512,256]{0,1:T(8,128)(2,1)} async-done(((bf16[4096,256]{0,1:T(8,128)(2,1)}), bf16[512,256]{0,1:T(8,128)(2,1)}) %reduce-scatter.3.cloned.1.call-update) | async-done | bytes 262160 | tf_op jit(solution)/shard_map/reduce_scatter | solution.py:111
  184.5 53.1 %reduce-scatter.5.cloned.1.call-done = bf16[512,256]{0,1:T(8,128)(2,1)} async-done(((bf16[4096,256]{0,1:T(8,128)(2,1)}), bf16[512,256]{0,1:T(8,128)(2,1)}) %reduce-scatter.5.cloned.1.call-update) | async-done | bytes 262160 | tf_op jit(solution)/shard_map/reduce_scatter | solution.py:111
  239.4 10.3 %bitcast_convert_fusion = bf16[512,8192]{1,0:T(8,128)(2,1)} fusion(bf16[512,2,256]{2,0,1:T(8,128)(2,1)S(1)} %reshape.173, bf16[8192,2,256]{2,1,0:T(2,128)(2,1)} %bitcast.216), kind=kOutput, calls=%fused_computation.10 | convolution fusion | flops 4299161600 | bytes 17301504 | tf_op jit(solution)/shard_map/dot_general | solution.py:125
  249.8 4.6 %dynamic-slice_bitcast_fusion = bf16[2,128,8192]{2,1,0:T(8,128)(2,1)} fusion(bf16[2,2,128,8192]{3,2,1,0:T(8,128)(2,1)} %bitcast.190, s32[]{:T(128)S(6)} %select_n.41), kind=kLoop, calls=%fused_computation.46 | loop fusion | bytes 8388612 | tf_op jit(solution)/shard_map/jit(dynamic_index_in_dim)/squeeze | solution.py:137
  255.5 7.1 %collective-permute-done = bf16[2,128,8192]{2,1,0:T(8,128)(2,1)} collective-permute-done((bf16[2,128,8192]{2,1,0:T(8,128)(2,1)}, bf16[2,128,8192]{2,1,0:T(8,128)(2,1)}, u32[]{:S(2)}, u32[]{:S(2)}) %collective-permute-start) | collective-permute-done | bytes 4194336 | tf_op jit(solution)/shard_map/ppermute | solution.py:139
  262.6 4.9 %convert_add_fusion = f32[2,128,8192]{2,1,0:T(8,128)S(1)} fusion(bf16[2,128,8192]{2,1,0:T(8,128)(2,1)} %collective-permute-done, bf16[2,2,128,8192]{3,2,1,0:T(8,128)(2,1)} %bitcast.191, s32[]{:T(128)S(6)} %select_n.40), kind=kLoop, calls=%fused_computation.21 | loop fusion | flops 6291456 | bytes 16777220 | tf_op jit(solution)/shard_map/add | solution.py:140
  267.6 3.3 copy-done
  270.9 1.6 fusion.26
  272.4 2.4 collective-permute-start.1
  275.0 5.0 %fusion.32 = bf16[128,1,8,128]{0,3,2,1:T(8,128)(2,1)S(1)} fusion(bf16[128,8,4224]{0,2,1:T(8,128)(2,1)} %fusion.3, bf16[128,128]{1,0:T(8,128)(2,1)S(1)} %copy-done.25, bf16[4096,128]{1,0:T(8,128)(2,1)S(1)} %copy-done.8), kind=kOutput, calls=%fused_computation.60 | convolution fusion | flops 1109721088 | bytes 9994240 | tf_op jit(solution)/shard_map/rgk,kd->rgd/dot_general | solution.py:46
  280.0 41.1 %collective-permute-done.1 = bf16[128,8192]{1,0:T(8,128)(2,1)} collective-permute-done((bf16[128,8192]{1,0:T(8,128)(2,1)}, bf16[128,8192]{1,0:T(8,128)(2,1)}, u32[]{:S(2)}, u32[]{:S(2)}) %collective-permute-start.1) | collective-permute-done | bytes 2097184 | tf_op jit(solution)/shard_map/ppermute | solution.py:144
  321.1 3.0 fusion.21
  324.2 4.7 %fusion.58 = bf16[128,8192]{1,0:T(8,128)(2,1)} fusion(f32[128]{0:T(128)S(1)} %broadcast_multiply_fusion, f32[128]{0:T(128)S(1)} %get-tuple-element.49, bf16[1,128,8192]{2,1,0:T(8,128)(2,1)S(1)} %copy-done.2, bf16[128,8192]{1,0:T(8,128)(2,1)} %collective-permute-done.1, f32[2,128,8192]{2,1,0:T(8,128)S(1)} %copy-done.1, s32[]{:T(128)S(6)} %select_n.43, ...), kind=kLoop, calls=%fused_computation.117 | loop fusion | flops 9437184 | bytes 10520068 | tf_op jit(solution)/shard_map/convert_element_type | solution.py:153
  328.9 2.1 collective-permute-start.4
  331.0 1.3 collective-permute-start.3
  332.3 1.9 collective-permute-start.2
  334.3 1.4 fusion.31
  339.0 5.4 %all-to-all-start.2 = ((bf16[4,128,512]{1,2,0:T(8,128)(2,1)}), bf16[4,128,512]{1,2,0:T(8,128)(2,1)S(1)}, u32[]{:S(2)}, u32[]{:S(2)}) async-start(bf16[4,128,512]{1,2,0:T(8,128)(2,1)} %copy_bitcast_fusion), calls=%async_computation.4 | async-start | bytes 1048576 | tf_op jit(solution)/shard_map/all_to_all | solution.py:118
  347.7 6.0 %all-to-all-done.2 = bf16[4,128,512]{1,2,0:T(8,128)(2,1)S(1)} async-done(((bf16[4,128,512]{1,2,0:T(8,128)(2,1)}), bf16[4,128,512]{1,2,0:T(8,128)(2,1)S(1)}, u32[]{:S(2)}, u32[]{:S(2)}) %all-to-all-start.2) | async-done | bytes 524320 | tf_op jit(solution)/shard_map/all_to_all | solution.py:118
  355.9 24.9 %collective-permute-done.3 = bf16[128,8192]{1,0:T(8,128)(2,1)} collective-permute-done((bf16[128,8192]{1,0:T(8,128)(2,1)}, bf16[128,8192]{1,0:T(8,128)(2,1)}, u32[]{:S(2)}, u32[]{:S(2)}) %collective-permute-start.3) | collective-permute-done | bytes 2097184 | tf_op jit(solution)/shard_map/ppermute | solution.py:157
  380.8 46.5 %collective-permute-done.2 = bf16[128,8192]{1,0:T(8,128)(2,1)} collective-permute-done((bf16[128,8192]{1,0:T(8,128)(2,1)}, bf16[128,8192]{1,0:T(8,128)(2,1)}, u32[]{:S(2)}, u32[]{:S(2)}) %collective-permute-start.2) | collective-permute-done | bytes 2097184 | tf_op jit(solution)/shard_map/ppermute | solution.py:157
  427.2 9.0 %add_bitcast_fusion = f32[1,128,8192]{2,1,0:T(8,128)} fusion(bf16[128,8192]{1,0:T(8,128)(2,1)} %collective-permute-done.4, bf16[128,8192]{1,0:T(8,128)(2,1)} %collective-permute-done.3, bf16[128,8192]{1,0:T(8,128)(2,1)} %collective-permute-done.2, f32[128]{0:T(128)S(1)} %broadcast_multiply_fusion, f32[128]{0:T(128)S(1)} %get-tuple-element.49, ...), kind=kLoop, calls=%fused_computation.44 | loop fusion | flops 14680064 | bytes 18908676 | tf_op jit(solution)/shard_map/broadcast_in_dim | solution.py:166
  (149 shorter events, 25.7 us)
Async XLA Ops:
  7.2 20.0 %copy-start.20 = (bf16[1,128,2048]{2,1,0:T(8,128)(2,1)S(1)}, bf16[1,128,2048]{2,1,0:T(8,128)(2,1)}, u32[]{:S(2)}) copy-start(bf16[1,128,2048]{2,1,0:T(8,128)(2,1)} %param.12) | copy-start | bytes 1572868
  7.2 20.3 %copy-start.21 = (bf16[1,128,2048]{2,1,0:T(8,128)(2,1)S(1)}, bf16[1,128,2048]{2,1,0:T(8,128)(2,1)}, u32[]{:S(2)}) copy-start(bf16[1,128,2048]{2,1,0:T(8,128)(2,1)} %param.15) | copy-start | bytes 1572868
  7.2 66.8 %all-gather.3.cloned.1.call-start = ((), (), s32[]{:S(2)}) async-start(), calls=%async_computation.5 | async-start | bytes 2359296 | tf_op jit(solution)/shard_map/all_gather | solution.py:94
  10.3 18.5 %copy-start.30 = (s32[1,128]{1,0:T(1,128)S(1)}, s32[1,128]{1,0:T(1,128)}, u32[]{:S(2)}) copy-start(s32[1,128]{1,0:T(1,128)} %param.21) | copy-start | bytes 1540
  10.3 18.5 %copy-start.32 = (s32[1,2]{1,0:T(1,128)S(1)}, s32[1,2]{1,0:T(1,128)}, u32[]{:S(2)}) copy-start(s32[1,2]{1,0:T(1,128)} %param.22) | copy-start | bytes 28
  10.3 18.6 %copy-start.31 = (s32[3,16]{1,0:T(4,128)S(1)}, s32[3,16]{1,0:T(4,128)}, u32[]{:S(2)}) copy-start(s32[3,16]{1,0:T(4,128)} %param.23) | copy-start | bytes 580
  10.3 18.9 %copy-start.26 = (bf16[1,128,256]{2,1,0:T(8,128)(2,1)S(1)}, bf16[1,128,256]{2,1,0:T(8,128)(2,1)}, u32[]{:S(2)}) copy-start(bf16[1,128,256]{2,1,0:T(8,128)(2,1)} %param.13) | copy-start | bytes 196612
  22.8 11.0 %all-to-all-start.1 = ((bf16[4,128,256]{2,1,0:T(8,128)(2,1)}), bf16[4,128,256]{2,1,0:T(8,128)(2,1)S(1)}, u32[]{:S(2)}, u32[]{:S(2)}) async-start(bf16[4,128,256]{2,1,0:T(8,128)(2,1)} %maximum_bitcast_fusion.13), calls=%async_computation.1 | async-start | bytes 524288 | tf_op jit(solution)/shard_map/all_to_all | solution.py:92
  27.2 101.2 %all-gather.5.cloned.1.call-start = ((), (), s32[]{:S(2)}) async-start(), calls=%async_computation.6 | async-start | bytes 2359296 | tf_op jit(solution)/shard_map/all_gather | solution.py:94
  34.5 43.1 %copy-start.24 = (bf16[128,128]{1,0:T(8,128)(2,1)S(1)}, bf16[128,128]{1,0:T(8,128)(2,1)}, u32[]{:S(2)}) copy-start(bf16[128,128]{1,0:T(8,128)(2,1)} %get-tuple-element.46) | copy-start | bytes 98308
  34.5 149.1 %reduce-scatter.3.cloned.1.call-start = ((), (), s32[]{:S(2)}) async-start(), calls=%async_computation.7 | async-start | bytes 2359296 | tf_op jit(solution)/shard_map/reduce_scatter | solution.py:111
  90.8 12.0 %copy-start.19 = (bf16[4096,128]{1,0:T(8,128)(2,1)S(1)}, bf16[4096,128]{1,0:T(8,128)(2,1)}, u32[]{:S(2)}) copy-start(bf16[4096,128]{1,0:T(8,128)(2,1)} %get-tuple-element.32) | copy-start | bytes 3145732
  90.8 12.0 %copy-start.22 = (bf16[128,1,8,128]{3,0,2,1:T(8,128)(2,1)S(1)}, bf16[128,1,8,128]{3,0,2,1:T(8,128)(2,1)}, u32[]{:S(2)}) copy-start(bf16[128,1,8,128]{3,0,2,1:T(8,128)(2,1)} %copy.183) | copy-start | bytes 786436
  90.8 12.0 %copy-start.29 = (bf16[128,128]{1,0:T(8,128)(2,1)S(1)}, bf16[128,128]{1,0:T(8,128)(2,1)}, u32[]{:S(2)}) copy-start(bf16[128,128]{1,0:T(8,128)(2,1)} %get-tuple-element.44) | copy-start | bytes 98308
  90.8 14.5 %slice-start.5 = ((s8[17301504]{0:T(1024)(128)(4,1)}), s8[4194304]{0:T(1024)(128)(4,1)S(1)}, s32[]{:S(2)}) async-start(s8[17301504]{0:T(1024)(128)(4,1)} %bitcast.188), calls=%async_computation.14 | async-start | bytes 8388608
  90.8 14.5 %slice-start.6 = ((s8[17301504]{0:T(1024)(128)(4,1)}), s8[4194304]{0:T(1024)(128)(4,1)S(1)}, s32[]{:S(2)}) async-start(s8[17301504]{0:T(1024)(128)(4,1)} %bitcast.188), calls=%async_computation.15 | async-start | bytes 8388608
  90.8 14.5 %slice-start.7 = ((s8[17301504]{0:T(1024)(128)(4,1)}), s8[4194304]{0:T(1024)(128)(4,1)S(1)}, s32[]{:S(2)}) async-start(s8[17301504]{0:T(1024)(128)(4,1)} %bitcast.188), calls=%async_computation.16 | async-start | bytes 8388608
  90.8 14.5 %slice-start.8 = ((s8[17301504]{0:T(1024)(128)(4,1)}), s8[4194304]{0:T(1024)(128)(4,1)S(1)}, s32[]{:S(2)}) async-start(s8[17301504]{0:T(1024)(128)(4,1)} %bitcast.188), calls=%async_computation.17 | async-start | bytes 8388608
  98.3 4.4 copy-start.5
  111.6 6.6 %copy-start.6 = (bf16[128,8,4224]{0,2,1:T(8,128)(2,1)S(1)}, bf16[128,8,4224]{0,2,1:T(8,128)(2,1)}, u32[]{:S(2)}) copy-start(bf16[128,8,4224]{0,2,1:T(8,128)(2,1)} %copy-done.5) | copy-start | bytes 25952260
  123.7 8.3 %copy-start.23 = (bf16[128,128]{1,0:T(8,128)(2,1)S(1)}, bf16[128,128]{1,0:T(8,128)(2,1)}, u32[]{:S(2)}) copy-start(bf16[128,128]{1,0:T(8,128)(2,1)} %get-tuple-element.47) | copy-start | bytes 98308
  123.8 113.9 %reduce-scatter.5.cloned.1.call-start = ((), (), s32[]{:S(2)}) async-start(), calls=%async_computation.8 | async-start | bytes 2359296 | tf_op jit(solution)/shard_map/reduce_scatter | solution.py:111
  144.8 12.0 %copy-start.18 = (bf16[4096,128]{1,0:T(8,128)(2,1)S(1)}, bf16[4096,128]{1,0:T(8,128)(2,1)}, u32[]{:S(2)}) copy-start(bf16[4096,128]{1,0:T(8,128)(2,1)} %get-tuple-element.34) | copy-start | bytes 3145732
  144.8 12.0 %copy-start.28 = (bf16[128,128]{1,0:T(8,128)(2,1)S(1)}, bf16[128,128]{1,0:T(8,128)(2,1)}, u32[]{:S(2)}) copy-start(bf16[128,128]{1,0:T(8,128)(2,1)} %get-tuple-element.45) | copy-start | bytes 98308
  144.8 14.5 %slice-start = ((s8[17301504]{0:T(1024)(128)(4,1)}), s8[4194304]{0:T(1024)(128)(4,1)S(1)}, s32[]{:S(2)}) async-start(s8[17301504]{0:T(1024)(128)(4,1)} %bitcast.186), calls=%async_computation.9 | async-start | bytes 8388608
  144.8 14.5 %slice-start.1 = ((s8[17301504]{0:T(1024)(128)(4,1)}), s8[4194304]{0:T(1024)(128)(4,1)S(1)}, s32[]{:S(2)}) async-start(s8[17301504]{0:T(1024)(128)(4,1)} %bitcast.186), calls=%async_computation.10 | async-start | bytes 8388608
  144.8 14.5 %slice-start.2 = ((s8[17301504]{0:T(1024)(128)(4,1)}), s8[4194304]{0:T(1024)(128)(4,1)S(1)}, s32[]{:S(2)}) async-start(s8[17301504]{0:T(1024)(128)(4,1)} %bitcast.186), calls=%async_computation.11 | async-start | bytes 8388608
  144.8 14.5 %slice-start.3 = ((s8[17301504]{0:T(1024)(128)(4,1)}), s8[4194304]{0:T(1024)(128)(4,1)S(1)}, s32[]{:S(2)}) async-start(s8[17301504]{0:T(1024)(128)(4,1)} %bitcast.186), calls=%async_computation.12 | async-start | bytes 8388608
  152.4 4.4 copy-start.3
  165.6 7.6 %copy-start.4 = (bf16[128,8,4224]{0,2,1:T(8,128)(2,1)S(1)}, bf16[128,8,4224]{0,2,1:T(8,128)(2,1)}, u32[]{:S(2)}) copy-start(bf16[128,8,4224]{0,2,1:T(8,128)(2,1)} %copy-done.3) | copy-start | bytes 25952260
  238.7 11.1 %copy-start.11 = (bf16[512,512]{0,1:T(8,128)(2,1)}, bf16[512,512]{0,1:T(8,128)(2,1)S(1)}, u32[]{:S(2)}) copy-start(bf16[512,512]{0,1:T(8,128)(2,1)S(1)} %constant_dynamic-update-slice_fusion) | copy-start | bytes 1572868
  254.4 8.2 %collective-permute-start = (bf16[2,128,8192]{2,1,0:T(8,128)(2,1)}, bf16[2,128,8192]{2,1,0:T(8,128)(2,1)}, u32[]{:S(2)}, u32[]{:S(2)}) collective-permute-start(bf16[2,128,8192]{2,1,0:T(8,128)(2,1)} %dynamic-slice_bitcast_fusion), channel_id=1, source_target_pairs={{0,1},{1,0},{2,3},{3,2},{4,5},{5,4},{6,7},{7,6},{8,9},{9,8},{10,11... | collective-permute-start | bytes 12582920 | tf_op jit(solution)/shard_map/ppermute | solution.py:139
  267.6 3.3 copy-start
  270.8 4.0 copy-start.27
  270.8 4.1 copy-start.8
  270.9 4.1 copy-start.25
  272.4 48.7 %collective-permute-start.1 = (bf16[128,8192]{1,0:T(8,128)(2,1)}, bf16[128,8192]{1,0:T(8,128)(2,1)}, u32[]{:S(2)}, u32[]{:S(2)}) collective-permute-start(bf16[128,8192]{1,0:T(8,128)(2,1)} %fusion.26), channel_id=1, source_target_pairs={{0,2},{1,3},{2,0},{3,1},{4,6},{5,7},{6,4},{7,5},{8,10},{9,11},{10,... | collective-permute-start | bytes 6291464 | tf_op jit(solution)/shard_map/ppermute | solution.py:144
  274.9 46.2 %copy-start.1 = (f32[2,128,8192]{2,1,0:T(8,128)S(1)}, f32[2,128,8192]{2,1,0:T(8,128)}, u32[]{:S(2)}) copy-start(f32[2,128,8192]{2,1,0:T(8,128)} %copy-done) | copy-start | bytes 25165828
  274.9 46.2 %copy-start.2 = (bf16[1,128,8192]{2,1,0:T(8,128)(2,1)S(1)}, bf16[1,128,8192]{2,1,0:T(8,128)(2,1)}, u32[]{:S(2)}) copy-start(bf16[1,128,8192]{2,1,0:T(8,128)(2,1)} %param.19) | copy-start | bytes 6291460
  321.1 13.2 %slice-start.10 = ((s8[8650752]{0:T(1024)(128)(4,1)}), s8[4194304]{0:T(1024)(128)(4,1)S(1)}, s32[]{:S(2)}) async-start(s8[8650752]{0:T(1024)(128)(4,1)} %bitcast.218), calls=%async_computation.19 | async-start | bytes 8388608
  321.1 13.2 %slice-start.11 = ((s8[8650752]{0:T(1024)(128)(4,1)}), s8[4194304]{0:T(1024)(128)(4,1)S(1)}, s32[]{:S(2)}) async-start(s8[8650752]{0:T(1024)(128)(4,1)} %bitcast.218), calls=%async_computation.20 | async-start | bytes 8388608
  324.2 10.1 %copy-start.10 = (bf16[4096,128]{1,0:T(8,128)(2,1)S(1)}, bf16[4096,128]{1,0:T(8,128)(2,1)}, u32[]{:S(2)}) copy-start(bf16[4096,128]{1,0:T(8,128)(2,1)} %copy-done.9) | copy-start | bytes 3145732
  324.2 10.1 %slice-start.12 = ((s8[8650752]{0:T(1024)(128)(4,1)}), s8[262144]{0:T(1024)(128)(4,1)S(1)}, s32[]{:S(2)}) async-start(s8[8650752]{0:T(1024)(128)(4,1)} %bitcast.218), calls=%async_computation.21 | async-start | bytes 524288
  328.9 9.2 %copy-start.12 = (bf16[512,512]{0,1:T(8,128)(2,1)S(1)}, bf16[512,512]{0,1:T(8,128)(2,1)}, u32[]{:S(2)}) copy-start(bf16[512,512]{0,1:T(8,128)(2,1)} %copy-done.11) | copy-start | bytes 1572868
  328.9 27.0 %collective-permute-start.4 = (bf16[128,8192]{1,0:T(8,128)(2,1)}, bf16[128,8192]{1,0:T(8,128)(2,1)}, u32[]{:S(2)}, u32[]{:S(2)}) collective-permute-start(bf16[128,8192]{1,0:T(8,128)(2,1)} %fusion.58), channel_id=1, source_target_pairs={{96,0},{97,1},{98,2},{99,3},{100,4},{101,5},{102,6},{103,7},{104,8... | collective-permute-start | bytes 6291464 | tf_op jit(solution)/shard_map/ppermute | solution.py:157
  331.0 49.7 %collective-permute-start.3 = (bf16[128,8192]{1,0:T(8,128)(2,1)}, bf16[128,8192]{1,0:T(8,128)(2,1)}, u32[]{:S(2)}, u32[]{:S(2)}) collective-permute-start(bf16[128,8192]{1,0:T(8,128)(2,1)} %fusion.58), channel_id=1, source_target_pairs={{64,0},{96,32},{65,1},{97,33},{66,2},{98,34},{67,3},{99,35},{68,4}... | collective-permute-start | bytes 6291464 | tf_op jit(solution)/shard_map/ppermute | solution.py:157
  332.3 94.9 %collective-permute-start.2 = (bf16[128,8192]{1,0:T(8,128)(2,1)}, bf16[128,8192]{1,0:T(8,128)(2,1)}, u32[]{:S(2)}, u32[]{:S(2)}) collective-permute-start(bf16[128,8192]{1,0:T(8,128)(2,1)} %fusion.58), channel_id=1, source_target_pairs={{32,0},{64,32},{96,64},{33,1},{65,33},{97,65},{34,2},{66,34},{98,6... | collective-permute-start | bytes 6291464 | tf_op jit(solution)/shard_map/ppermute | solution.py:157
  339.0 14.8 %all-to-all-start.2 = ((bf16[4,128,512]{1,2,0:T(8,128)(2,1)}), bf16[4,128,512]{1,2,0:T(8,128)(2,1)S(1)}, u32[]{:S(2)}, u32[]{:S(2)}) async-start(bf16[4,128,512]{1,2,0:T(8,128)(2,1)} %copy_bitcast_fusion), calls=%async_computation.4 | async-start | bytes 1048576 | tf_op jit(solution)/shard_map/all_to_all | solution.py:118
  (9 other events, 14.1 us)
Sparse Core Ops, SparseCore 0:
  22.1 51.7 all-gather.2
  76.2 52.1 all-gather.4
  131.3 52.1 reduce-scatter.2
  185.8 51.8 reduce-scatter.4
where the time goes:
time: 448 us; the launch traced here: 443 us
  waiting for transfers between devices  230 us (51%)
  other arithmetic  62.3 us (14%)
  matrix products  57.7 us (13%)
  local copies, waits for them, and re-layouts  48.1 us (11%)
  starting transfers between devices  18.8 us (4%)
  between operations  14.8 us (3%)
  blocking collectives  11.5 us (3%)
    ppermute x3, waiting for transfers between devices, on_device(): lax.ppermute(term_low, 'section', pairs).astype(jnp.float32)  71.3 us
    reduce_scatter x2, waiting for transfers between devices, on_device(): lax.psum_scatter(pool_grad, 'sample', scatter_dimension=0, tiled=True)  57.8 us
    all_gather x2, waiting for transfers between devices, on_device(): pool = lax.all_gather(got, 'sample', axis=0, tiled=True)  44 us
    ppermute x1, waiting for transfers between devices, on_device(): got2 = lax.ppermute(other.astype(jnp.bfloat16), 'tensor', chip_pairs)  41.1 us
    unnamed x100, local copies, waits for them, and re-layouts  23.1 us
    sub x2, other arithmetic, attend_group(): exponent = jnp.exp(scores - row_max)  21.1 us
    convert_element_type x2, other arithmetic, attend_group(): weights_low = softmax_w.astype(jnp.bfloat16)  15.1 us
    dot_general x2, matrix products, attend_group(): jnp.einsum('rgk,rgd->kd', score_grad, query_grp, preferred_element_type=j...  13 us
  transfers between devices with their start and end apart: 11, of which 10 were waited for; matrix products, arithmetic and copies ran while one was open for 24% of the time, Pallas kernels for 0%

commit v1 on v0

--- a/solution.py
+++ b/solution.py
@@ -7,6 +7,18 @@
 PAGE = 128
 MASKED_SCORE = -1e30
 EPSILON = 1e-05
+
+
+def loads_change(target, where_dim):
+    return jnp.concatenate(
+        jax.lax.all_to_all(
+            jnp.stack([target for _ in range(jax.lax.axis_size("sample"))]),
+            axis_name="sample",
+            split_axis=0,
+            concat_axis=0,
+        ),
+        axis=where_dim,
+    )
 
 
 def visible_keys(seg_row, prompt_row, table, pooled_rows):
@@ -91,7 +103,7 @@
             send = send.transpose(1, 0, 2)
             got = lax.all_to_all(send, "tensor", 0, 0, tiled=True)
             got = got.reshape(block_rows, 2 * HEAD_SIZE)
-            pool = lax.all_gather(got, "sample", axis=0, tiled=True)
+            pool = loads_change(got, 0)
             key_rows = jnp.concatenate(
                 [pool[:, :HEAD_SIZE], own_keys[:, low_col : low_col + HEAD_SIZE]], axis=0
             )

time: 448 us -> 463 us (1.033)
  starting transfers between devices: 18.8 us -> 33.5 us
  blocking collectives: 11.5 us -> 0 us
  waiting for transfers between devices: 230 us -> 236 us
  matrix products: 57.7 us -> 62.4 us
    all_gather x2 -> x0, waiting for transfers between devices: 44 us -> none  [on_device(): pool = lax.all_gather(got, 'sample', axis=0, tiled=True)]
    all_to_all x0 -> x2, waiting for transfers between devices: none -> 40.5 us  [loads_change(): jax.lax.all_to_all(jnp.stack([target for _ in range(jax.lax.axis_size('sa...]
    all_to_all x1 -> x0, blocking collectives: 11.5 us -> none  [on_device(): got = lax.all_to_all(send, 'tensor', 0, 0, tiled=True)]
    all_to_all x1 -> x2, waiting for transfers between devices: 2.29 us -> 12.2 us  [on_device(): got = lax.all_to_all(send, 'tensor', 0, 0, tiled=True)]
    all_to_all x0 -> x2, starting transfers between devices: none -> 9.63 us  [loads_change(): jax.lax.all_to_all(jnp.stack([target for _ in range(jax.lax.axis_size('sa...]
    all_to_all x1 -> x2, starting transfers between devices: 4.41 us -> 9.48 us  [on_device(): got = lax.all_to_all(send, 'tensor', 0, 0, tiled=True)]
  transfers between devices with their start and end apart: 11 -> 12, of which waited for: 10 -> 11; matrix products, arithmetic and copies ran while one was open for 24% -> 15% of each run, Pallas kernels for 0% -> 0%
where the time goes in v1:
time: 463 us; the launch traced here: 458 us
  waiting for transfers between devices  236 us (51%)
  other arithmetic  63.2 us (14%)
  matrix products  62.4 us (13%)
  local copies, waits for them, and re-layouts  47.4 us (10%)
  starting transfers between devices  33.5 us (7%)
  between operations  15 us (3%)
    ppermute x3, waiting for transfers between devices, on_device(): lax.ppermute(term_low, 'section', pairs).astype(jnp.float32)  72 us
    reduce_scatter x2, waiting for transfers between devices, on_device(): lax.psum_scatter(pool_grad, 'sample', scatter_dimension=0, tiled=True)  57.4 us
    ppermute x1, waiting for transfers between devices, on_device(): got2 = lax.ppermute(other.astype(jnp.bfloat16), 'tensor', chip_pairs)  40.9 us
    all_to_all x2, waiting for transfers between devices, loads_change(): jax.lax.all_to_all(jnp.stack([target for _ in range(jax.lax.axis_size('sa...  40.5 us
    unnamed x100, local copies, waits for them, and re-layouts  23 us
    sub x2, other arithmetic, attend_group(): exponent = jnp.exp(scores - row_max)  21.1 us
    convert_element_type x2, other arithmetic, attend_group(): weights_low = softmax_w.astype(jnp.bfloat16)  14.3 us
    dot_general x2, matrix products, attend_group(): jnp.einsum('rgd,kd->rgk', grad_grp, value_rows, preferred_element_type=jn...  14.2 us
  transfers between devices with their start and end apart: 12, of which 11 were waited for; matrix products, arithmetic and copies ran while one was open for 15% of the time, Pallas kernels for 0%

profile of v1, /device:TPU:3, one launch (start us, length us, event | category | flops | bytes accessed | tf_op | source)
XLA Modules:
  0.0 457.6 jit_solution(6521664231095195686)
XLA Ops:
  10.2 5.1 %all-to-all-start.2 = ((bf16[4,128,256]{1,2,0:T(8,128)(2,1)}), bf16[4,128,256]{1,2,0:T(8,128)(2,1)S(1)}, u32[]{:S(2)}, u32[]{:S(2)}) async-start(bf16[4,128,256]{1,2,0:T(8,128)(2,1)} %maximum_bitcast_fusion.13), calls=%async_computation.2 | async-start | bytes 524288 | tf_op jit(solution)/shard_map/all_to_all | solution.py:104
  16.0 5.8 %all-to-all-done.2 = bf16[4,128,256]{1,2,0:T(8,128)(2,1)S(1)} async-done(((bf16[4,128,256]{1,2,0:T(8,128)(2,1)}), bf16[4,128,256]{1,2,0:T(8,128)(2,1)S(1)}, u32[]{:S(2)}, u32[]{:S(2)}) %all-to-all-start.2) | async-done | bytes 262176 | tf_op jit(solution)/shard_map/all_to_all | solution.py:104
  21.9 4.3 all-to-all-start
  26.4 6.4 %all-to-all-done = bf16[4,128,256]{1,2,0:T(8,128)(2,1)S(1)} async-done(((bf16[4,128,256]{1,2,0:T(8,128)(2,1)}), bf16[4,128,256]{1,2,0:T(8,128)(2,1)S(1)}, u32[]{:S(2)}, u32[]{:S(2)}) %all-to-all-start) | async-done | bytes 262176 | tf_op jit(solution)/shard_map/all_to_all | solution.py:104
  34.2 5.1 %all-to-all-start.3 = ((bf16[8,512,256]{2,1,0:T(8,128)(2,1)}), bf16[8,512,256]{2,1,0:T(8,128)(2,1)S(1)}, u32[]{:S(2)}, u32[]{:S(2)}) async-start(bf16[8,512,256]{2,1,0:T(8,128)(2,1)} %stack.20), calls=%async_computation.3 | async-start | bytes 4194304 | tf_op jit(solution)/shard_map/all_to_all | solution.py:14
  43.0 22.2 %all-to-all-done.3 = bf16[8,512,256]{2,1,0:T(8,128)(2,1)S(1)} async-done(((bf16[8,512,256]{2,1,0:T(8,128)(2,1)}), bf16[8,512,256]{2,1,0:T(8,128)(2,1)S(1)}, u32[]{:S(2)}, u32[]{:S(2)}) %all-to-all-start.3) | async-done | bytes 2097184 | tf_op jit(solution)/shard_map/all_to_all | solution.py:14
  65.2 1.6 stack.18
  66.8 4.5 all-to-all-start.1
  71.4 2.0 copy.161
  75.4 2.6 fusion.60
  78.0 18.2 %all-to-all-done.1 = bf16[8,512,256]{2,1,0:T(8,128)(2,1)} async-done(((bf16[8,512,256]{2,1,0:T(8,128)(2,1)}), bf16[8,512,256]{2,1,0:T(8,128)(2,1)}, u32[]{:S(2)}, u32[]{:S(2)}) %all-to-all-start.1) | async-done | bytes 2097184 | tf_op jit(solution)/shard_map/all_to_all | solution.py:14
  96.3 2.6 fusion.59
  99.9 3.3 fusion.34
  103.2 10.7 %fusion.66 = (f32[128,8]{0,1:T(8,128)S(1)}, f32[128,8,4224]{0,2,1:T(8,128)}) fusion(f32[4224,128,8]{1,0,2:T(8,128)S(1)} %fusion.34, pred[128,4224]{0,1:T(8,128)(4,1)S(1)} %pad_add_fusion), kind=kOutput, calls=%fused_computation.125 | output fusion | flops 17305728 | bytes 35147776 | tf_op jit(solution)/shard_map/sub | solution.py:46
  114.0 6.8 %fusion.13 = bf16[128,8,4224]{0,2,1:T(8,128)(2,1)S(1)} fusion(f32[128,8,4224]{0,2,1:T(8,128)} %get-tuple-element.59, f32[128,8]{0,1:T(8,128)S(1)} %get-tuple-element.58), kind=kLoop, calls=%fused_computation.23 | loop fusion | flops 8650752 | bytes 25956352 | tf_op jit(solution)/shard_map/convert_element_type | solution.py:48
  120.8 3.8 fusion.19
  124.6 2.5 fusion.29
  127.5 7.1 %fusion.3 = bf16[128,8,4224]{0,2,1:T(8,128)(2,1)} fusion(f32[128,8]{0,1:T(8,128)S(1)} %fusion.29, f32[128,8,4224]{0,2,1:T(8,128)S(1)} %bitcast.191, f32[128,8]{0,1:T(8,128)S(1)} %get-tuple-element.58, bf16[128,128]{1,0:T(8,128)(2,1)S(1)} %get-tuple-element.50, bf16[4096,128]{1,0:T(8,128)(2,1)} %get-tuple-element.38, bf16[128,2,8,128]{0,3,2,1:T(8,128)(2,1)} %bitcast.204), kind=kOutput, calls=%fused_computation.6 | convolution fusion | flops 1126760448 | bytes 27303936 | tf_op jit(solution)/shard_map/rgd,kd->rgk/dot_general | solution.py:53
  134.6 6.4 %fusion.17 = bf16[4224,128]{0,1:T(8,128)(2,1)S(1)} fusion(bf16[128,8,4224]{0,2,1:T(8,128)(2,1)} %fusion.3, bf16[128,2,8,128]{0,3,2,1:T(8,128)(2,1)} %bitcast.199), kind=kOutput, calls=%fused_computation.34 | convolution fusion | flops 1108377600 | bytes 9994240 | tf_op jit(solution)/shard_map/rgk,rgd->kd/dot_general | solution.py:62
  143.3 1.5 pad_maximum_fusion
  144.9 3.4 fusion.33
  148.2 10.4 %fusion.65 = (f32[128,8]{0,1:T(8,128)S(1)}, f32[128,8,4224]{0,2,1:T(8,128)}) fusion(f32[4224,128,8]{1,0,2:T(8,128)S(1)} %fusion.33, pred[128,4224]{0,1:T(8,128)(4,1)S(1)} %pad_add_fusion), kind=kOutput, calls=%fused_computation.124 | output fusion | flops 17305728 | bytes 35147776 | tf_op jit(solution)/shard_map/sub | solution.py:46
  158.7 7.6 %fusion.14 = bf16[128,8,4224]{0,2,1:T(8,128)(2,1)S(1)} fusion(f32[128,8,4224]{0,2,1:T(8,128)} %get-tuple-element.57, f32[128,8]{0,1:T(8,128)S(1)} %get-tuple-element.56), kind=kLoop, calls=%fused_computation.24 | loop fusion | flops 8650752 | bytes 25956352 | tf_op jit(solution)/shard_map/convert_element_type | solution.py:48
  166.2 4.4 copy-done.3
  170.6 2.5 fusion.30
  173.4 7.1 %fusion.2 = bf16[128,8,4224]{0,2,1:T(8,128)(2,1)} fusion(f32[128,8]{0,1:T(8,128)S(1)} %fusion.30, f32[128,8,4224]{0,2,1:T(8,128)S(1)} %bitcast.193, f32[128,8]{0,1:T(8,128)S(1)} %get-tuple-element.56, bf16[128,128]{1,0:T(8,128)(2,1)S(1)} %get-tuple-element.51, bf16[4096,128]{1,0:T(8,128)(2,1)} %get-tuple-element.40, bf16[128,2,8,128]{0,3,2,1:T(8,128)(2,1)} %bitcast.205), kind=kOutput, calls=%fused_computation.3 | convolution fusion | flops 1126760448 | bytes 27303936 | tf_op jit(solution)/shard_map/rgd,kd->rgk/dot_general | solution.py:53
  180.5 6.5 %fusion.18 = bf16[4224,128]{0,1:T(8,128)(2,1)S(1)} fusion(bf16[128,8,4224]{0,2,1:T(8,128)(2,1)} %fusion.2, bf16[128,2,8,128]{0,3,2,1:T(8,128)(2,1)S(1)} %bitcast.201), kind=kOutput, calls=%fused_computation.35 | convolution fusion | flops 1108377600 | bytes 9994240 | tf_op jit(solution)/shard_map/rgk,rgd->kd/dot_general | solution.py:62
  188.1 2.9 fusion.20
  193.7 4.1 reduce-scatter.3.cloned.1.call-done
  198.8 53.3 %reduce-scatter.5.cloned.1.call-done = bf16[512,256]{0,1:T(8,128)(2,1)} async-done(((bf16[4096,256]{0,1:T(8,128)(2,1)}), bf16[512,256]{0,1:T(8,128)(2,1)}) %reduce-scatter.5.cloned.1.call-update) | async-done | bytes 262160 | tf_op jit(solution)/shard_map/reduce_scatter | solution.py:123
  254.0 10.1 %bitcast_convert_fusion = bf16[512,8192]{1,0:T(8,128)(2,1)} fusion(bf16[512,2,256]{2,0,1:T(8,128)(2,1)S(1)} %reshape.177, bf16[8192,2,256]{2,1,0:T(2,128)(2,1)} %bitcast.223), kind=kOutput, calls=%fused_computation.10 | convolution fusion | flops 4299161600 | bytes 17301504 | tf_op jit(solution)/shard_map/dot_general | solution.py:137
  264.2 4.6 %dynamic-slice_bitcast_fusion = bf16[2,128,8192]{2,1,0:T(8,128)(2,1)} fusion(bf16[2,2,128,8192]{3,2,1,0:T(8,128)(2,1)} %bitcast.194, s32[]{:T(128)S(6)} %select_n.41), kind=kLoop, calls=%fused_computation.46 | loop fusion | bytes 8388612 | tf_op jit(solution)/shard_map/jit(dynamic_index_in_dim)/squeeze | solution.py:149
  269.9 7.1 %collective-permute-done = bf16[2,128,8192]{2,1,0:T(8,128)(2,1)} collective-permute-done((bf16[2,128,8192]{2,1,0:T(8,128)(2,1)}, bf16[2,128,8192]{2,1,0:T(8,128)(2,1)}, u32[]{:S(2)}, u32[]{:S(2)}) %collective-permute-start) | collective-permute-done | bytes 4194336 | tf_op jit(solution)/shard_map/ppermute | solution.py:151
  277.0 4.9 %convert_add_fusion = f32[2,128,8192]{2,1,0:T(8,128)S(1)} fusion(bf16[2,128,8192]{2,1,0:T(8,128)(2,1)} %collective-permute-done, bf16[2,2,128,8192]{3,2,1,0:T(8,128)(2,1)} %bitcast.195, s32[]{:T(128)S(6)} %select_n.40), kind=kLoop, calls=%fused_computation.21 | loop fusion | flops 6291456 | bytes 16777220 | tf_op jit(solution)/shard_map/add | solution.py:152
  282.0 3.3 copy-done
  285.2 1.6 fusion.26
  286.8 2.5 collective-permute-start.1
  289.3 5.3 %fusion.32 = bf16[128,1,8,128]{0,3,2,1:T(8,128)(2,1)S(1)} fusion(bf16[128,8,4224]{0,2,1:T(8,128)(2,1)} %fusion.3, bf16[128,128]{1,0:T(8,128)(2,1)S(1)} %copy-done.23, bf16[4096,128]{1,0:T(8,128)(2,1)} %copy-done.6), kind=kOutput, calls=%fused_computation.60 | convolution fusion | flops 1109721088 | bytes 9994240 | tf_op jit(solution)/shard_map/rgk,kd->rgd/dot_general | solution.py:58
  294.6 40.9 %collective-permute-done.1 = bf16[128,8192]{1,0:T(8,128)(2,1)} collective-permute-done((bf16[128,8192]{1,0:T(8,128)(2,1)}, bf16[128,8192]{1,0:T(8,128)(2,1)}, u32[]{:S(2)}, u32[]{:S(2)}) %collective-permute-start.1) | collective-permute-done | bytes 2097184 | tf_op jit(solution)/shard_map/ppermute | solution.py:156
  335.5 3.0 fusion.21
  338.6 4.7 %fusion.58 = bf16[128,8192]{1,0:T(8,128)(2,1)} fusion(f32[128]{0:T(128)S(1)} %broadcast_multiply_fusion, f32[128]{0:T(128)S(1)} %get-tuple-element.55, bf16[1,128,8192]{2,1,0:T(8,128)(2,1)S(1)} %copy-done.2, bf16[128,8192]{1,0:T(8,128)(2,1)} %collective-permute-done.1, f32[2,128,8192]{2,1,0:T(8,128)S(1)} %copy-done.1, s32[]{:T(128)S(6)} %select_n.43, ...), kind=kLoop, calls=%fused_computation.117 | loop fusion | flops 9437184 | bytes 10520068 | tf_op jit(solution)/shard_map/convert_element_type | solution.py:165
  343.2 2.1 collective-permute-start.4
  346.7 1.9 collective-permute-start.2
  352.6 5.4 %all-to-all-start.4 = ((bf16[4,128,512]{1,2,0:T(8,128)(2,1)}), bf16[4,128,512]{1,2,0:T(8,128)(2,1)S(1)}, u32[]{:S(2)}, u32[]{:S(2)}) async-start(bf16[4,128,512]{1,2,0:T(8,128)(2,1)} %copy_bitcast_fusion), calls=%async_computation.6 | async-start | bytes 1048576 | tf_op jit(solution)/shard_map/all_to_all | solution.py:130
  361.3 6.0 %all-to-all-done.4 = bf16[4,128,512]{1,2,0:T(8,128)(2,1)S(1)} async-done(((bf16[4,128,512]{1,2,0:T(8,128)(2,1)}), bf16[4,128,512]{1,2,0:T(8,128)(2,1)S(1)}, u32[]{:S(2)}, u32[]{:S(2)}) %all-to-all-start.4) | async-done | bytes 524320 | tf_op jit(solution)/shard_map/all_to_all | solution.py:130
  369.5 25.6 %collective-permute-done.3 = bf16[128,8192]{1,0:T(8,128)(2,1)} collective-permute-done((bf16[128,8192]{1,0:T(8,128)(2,1)}, bf16[128,8192]{1,0:T(8,128)(2,1)}, u32[]{:S(2)}, u32[]{:S(2)}) %collective-permute-start.3) | collective-permute-done | bytes 2097184 | tf_op jit(solution)/shard_map/ppermute | solution.py:169
  395.1 46.5 %collective-permute-done.2 = bf16[128,8192]{1,0:T(8,128)(2,1)} collective-permute-done((bf16[128,8192]{1,0:T(8,128)(2,1)}, bf16[128,8192]{1,0:T(8,128)(2,1)}, u32[]{:S(2)}, u32[]{:S(2)}) %collective-permute-start.2) | collective-permute-done | bytes 2097184 | tf_op jit(solution)/shard_map/ppermute | solution.py:169
  441.6 9.0 %add_bitcast_fusion = f32[1,128,8192]{2,1,0:T(8,128)} fusion(bf16[128,8192]{1,0:T(8,128)(2,1)} %collective-permute-done.4, bf16[128,8192]{1,0:T(8,128)(2,1)} %collective-permute-done.3, bf16[128,8192]{1,0:T(8,128)(2,1)} %collective-permute-done.2, f32[128]{0:T(128)S(1)} %broadcast_multiply_fusion, f32[128]{0:T(128)S(1)} %get-tuple-element.55, ...), kind=kLoop, calls=%fused_computation.44 | loop fusion | flops 14680064 | bytes 18908676 | tf_op jit(solution)/shard_map/broadcast_in_dim | solution.py:178
  (148 shorter events, 33.1 us)
Async XLA Ops:
  10.2 11.7 %all-to-all-start.2 = ((bf16[4,128,256]{1,2,0:T(8,128)(2,1)}), bf16[4,128,256]{1,2,0:T(8,128)(2,1)S(1)}, u32[]{:S(2)}, u32[]{:S(2)}) async-start(bf16[4,128,256]{1,2,0:T(8,128)(2,1)} %maximum_bitcast_fusion.13), calls=%async_computation.2 | async-start | bytes 524288 | tf_op jit(solution)/shard_map/all_to_all | solution.py:104
  21.9 10.9 %all-to-all-start = ((bf16[4,128,256]{1,2,0:T(8,128)(2,1)}), bf16[4,128,256]{1,2,0:T(8,128)(2,1)S(1)}, u32[]{:S(2)}, u32[]{:S(2)}) async-start(bf16[4,128,256]{1,2,0:T(8,128)(2,1)} %maximum_bitcast_fusion.12), calls=%async_computation | async-start | bytes 524288 | tf_op jit(solution)/shard_map/all_to_all | solution.py:104
  26.2 14.5 %copy-start.27 = (s32[1,128]{1,0:T(1,128)S(1)}, s32[1,128]{1,0:T(1,128)}, u32[]{:S(2)}) copy-start(s32[1,128]{1,0:T(1,128)} %param.21) | copy-start | bytes 1540
  26.2 14.5 %copy-start.31 = (s32[1,2]{1,0:T(1,128)S(1)}, s32[1,2]{1,0:T(1,128)}, u32[]{:S(2)}) copy-start(s32[1,2]{1,0:T(1,128)} %param.22) | copy-start | bytes 28
  26.2 14.6 %copy-start.29 = (s32[3,16]{1,0:T(4,128)S(1)}, s32[3,16]{1,0:T(4,128)}, u32[]{:S(2)}) copy-start(s32[3,16]{1,0:T(4,128)} %param.23) | copy-start | bytes 580
  26.2 15.8 %copy-start.24 = (bf16[1,128,256]{2,1,0:T(8,128)(2,1)S(1)}, bf16[1,128,256]{2,1,0:T(8,128)(2,1)}, u32[]{:S(2)}) copy-start(bf16[1,128,256]{2,1,0:T(8,128)(2,1)} %param.13) | copy-start | bytes 196612
  34.2 31.0 %all-to-all-start.3 = ((bf16[8,512,256]{2,1,0:T(8,128)(2,1)}), bf16[8,512,256]{2,1,0:T(8,128)(2,1)S(1)}, u32[]{:S(2)}, u32[]{:S(2)}) async-start(bf16[8,512,256]{2,1,0:T(8,128)(2,1)} %stack.20), calls=%async_computation.3 | async-start | bytes 4194304 | tf_op jit(solution)/shard_map/all_to_all | solution.py:14
  40.7 32.8 %copy-start.11 = (bf16[1,128,2048]{1,2,0:T(8,128)(2,1)}, bf16[1,128,2048]{1,2,0:T(8,128)(2,1)S(1)}, u32[]{:S(2)}) copy-start(bf16[1,128,2048]{1,2,0:T(8,128)(2,1)S(1)} %copy.163) | copy-start | bytes 1572868
  42.0 56.9 %copy-start.22 = (bf16[128,128]{1,0:T(8,128)(2,1)}, bf16[128,128]{1,0:T(8,128)(2,1)S(1)}, u32[]{:S(2)}) copy-start(bf16[128,128]{1,0:T(8,128)(2,1)S(1)} %get-tuple-element.52) | copy-start | bytes 98308
  42.9 30.5 %copy-start.17 = (bf16[128,1,8,128]{0,3,2,1:T(8,128)(2,1)S(1)}, bf16[128,1,8,128]{0,3,2,1:T(8,128)(2,1)}, u32[]{:S(2)}) copy-start(bf16[128,1,8,128]{0,3,2,1:T(8,128)(2,1)} %get-tuple-element.44) | copy-start | bytes 786436
  65.2 10.0 %copy-start.5 = (bf16[8,512,256]{2,1,0:T(8,128)(2,1)}, bf16[8,512,256]{2,1,0:T(8,128)(2,1)S(1)}, u32[]{:S(2)}) copy-start(bf16[8,512,256]{2,1,0:T(8,128)(2,1)S(1)} %all-to-all-done.3) | copy-start | bytes 6291460
  65.2 10.0 %copy-start.25 = (bf16[1,128,256]{2,1,0:T(8,128)(2,1)S(1)}, bf16[1,128,256]{2,1,0:T(8,128)(2,1)}, u32[]{:S(2)}) copy-start(bf16[1,128,256]{2,1,0:T(8,128)(2,1)} %param.14) | copy-start | bytes 196612
  66.8 4.5 copy-start.28
  66.8 4.6 copy-start.30
  66.8 29.5 %all-to-all-start.1 = ((bf16[8,512,256]{2,1,0:T(8,128)(2,1)}), bf16[8,512,256]{2,1,0:T(8,128)(2,1)}, u32[]{:S(2)}, u32[]{:S(2)}) async-start(bf16[8,512,256]{2,1,0:T(8,128)(2,1)} %stack.18), calls=%async_computation.1 | async-start | bytes 4194304 | tf_op jit(solution)/shard_map/all_to_all | solution.py:14
  71.3 126.5 %reduce-scatter.3.cloned.1.call-start = ((), (), s32[]{:S(2)}) async-start(), calls=%async_computation.7 | async-start | bytes 2359296 | tf_op jit(solution)/shard_map/reduce_scatter | solution.py:123
  114.0 6.8 %copy-start.12 = (bf16[1,128,2048]{1,2,0:T(8,128)(2,1)S(1)}, bf16[1,128,2048]{1,2,0:T(8,128)(2,1)}, u32[]{:S(2)}) copy-start(bf16[1,128,2048]{1,2,0:T(8,128)(2,1)} %copy-done.11) | copy-start | bytes 1572868
  120.8 3.9 copy-start.19
  120.8 6.4 %slice-start = ((s8[17301504]{0:T(1024)(128)(4,1)}), s8[4194304]{0:T(1024)(128)(4,1)S(1)}, s32[]{:S(2)}) async-start(s8[17301504]{0:T(1024)(128)(4,1)} %bitcast.190), calls=%async_computation.9 | async-start | bytes 8388608
  120.8 6.4 %slice-start.1 = ((s8[17301504]{0:T(1024)(128)(4,1)}), s8[4194304]{0:T(1024)(128)(4,1)S(1)}, s32[]{:S(2)}) async-start(s8[17301504]{0:T(1024)(128)(4,1)} %bitcast.190), calls=%async_computation.10 | async-start | bytes 8388608
  120.8 6.4 %slice-start.2 = ((s8[17301504]{0:T(1024)(128)(4,1)}), s8[4194304]{0:T(1024)(128)(4,1)S(1)}, s32[]{:S(2)}) async-start(s8[17301504]{0:T(1024)(128)(4,1)} %bitcast.190), calls=%async_computation.11 | async-start | bytes 8388608
  144.8 107.2 %reduce-scatter.5.cloned.1.call-start = ((), (), s32[]{:S(2)}) async-start(), calls=%async_computation.8 | async-start | bytes 2359296 | tf_op jit(solution)/shard_map/reduce_scatter | solution.py:123
  158.6 12.0 %copy-start.18 = (bf16[4096,128]{1,0:T(8,128)(2,1)S(1)}, bf16[4096,128]{1,0:T(8,128)(2,1)}, u32[]{:S(2)}) copy-start(bf16[4096,128]{1,0:T(8,128)(2,1)} %get-tuple-element.40) | copy-start | bytes 3145732
  158.6 12.0 %copy-start.20 = (bf16[128,1,8,128]{3,0,2,1:T(8,128)(2,1)S(1)}, bf16[128,1,8,128]{3,0,2,1:T(8,128)(2,1)}, u32[]{:S(2)}) copy-start(bf16[128,1,8,128]{3,0,2,1:T(8,128)(2,1)} %copy.226) | copy-start | bytes 786436
  158.6 14.5 %slice-start.5 = ((s8[17301504]{0:T(1024)(128)(4,1)}), s8[4194304]{0:T(1024)(128)(4,1)S(1)}, s32[]{:S(2)}) async-start(s8[17301504]{0:T(1024)(128)(4,1)} %bitcast.192), calls=%async_computation.14 | async-start | bytes 8388608
  158.6 14.5 %slice-start.6 = ((s8[17301504]{0:T(1024)(128)(4,1)}), s8[4194304]{0:T(1024)(128)(4,1)S(1)}, s32[]{:S(2)}) async-start(s8[17301504]{0:T(1024)(128)(4,1)} %bitcast.192), calls=%async_computation.15 | async-start | bytes 8388608
  158.6 14.5 %slice-start.7 = ((s8[17301504]{0:T(1024)(128)(4,1)}), s8[4194304]{0:T(1024)(128)(4,1)S(1)}, s32[]{:S(2)}) async-start(s8[17301504]{0:T(1024)(128)(4,1)} %bitcast.192), calls=%async_computation.16 | async-start | bytes 8388608
  158.7 14.5 %slice-start.8 = ((s8[17301504]{0:T(1024)(128)(4,1)}), s8[4194304]{0:T(1024)(128)(4,1)S(1)}, s32[]{:S(2)}) async-start(s8[17301504]{0:T(1024)(128)(4,1)} %bitcast.192), calls=%async_computation.17 | async-start | bytes 8388608
  166.2 4.4 copy-start.3
  173.4 7.1 %copy-start.10 = (bf16[1,128,2048]{1,2,0:T(8,128)(2,1)S(1)}, bf16[1,128,2048]{1,2,0:T(8,128)(2,1)}, u32[]{:S(2)}) copy-start(bf16[1,128,2048]{1,2,0:T(8,128)(2,1)} %copy.161) | copy-start | bytes 1572868
  180.5 7.6 %copy-start.4 = (bf16[128,8,4224]{0,2,1:T(8,128)(2,1)S(1)}, bf16[128,8,4224]{0,2,1:T(8,128)(2,1)}, u32[]{:S(2)}) copy-start(bf16[128,8,4224]{0,2,1:T(8,128)(2,1)} %copy-done.3) | copy-start | bytes 25952260
  180.5 7.6 %copy-start.13 = (bf16[1,128,2048]{1,2,0:T(8,128)(2,1)S(1)}, bf16[1,128,2048]{1,2,0:T(8,128)(2,1)}, u32[]{:S(2)}) copy-start(bf16[1,128,2048]{1,2,0:T(8,128)(2,1)} %copy-done.11) | copy-start | bytes 1572868
  253.0 11.1 %copy-start.8 = (bf16[512,512]{0,1:T(8,128)(2,1)}, bf16[512,512]{0,1:T(8,128)(2,1)S(1)}, u32[]{:S(2)}) copy-start(bf16[512,512]{0,1:T(8,128)(2,1)S(1)} %constant_dynamic-update-slice_fusion) | copy-start | bytes 1572868
  268.8 8.2 %collective-permute-start = (bf16[2,128,8192]{2,1,0:T(8,128)(2,1)}, bf16[2,128,8192]{2,1,0:T(8,128)(2,1)}, u32[]{:S(2)}, u32[]{:S(2)}) collective-permute-start(bf16[2,128,8192]{2,1,0:T(8,128)(2,1)} %dynamic-slice_bitcast_fusion), channel_id=1, source_target_pairs={{0,1},{1,0},{2,3},{3,2},{4,5},{5,4},{6,7},{7,6},{8,9},{9,8},{10,11... | collective-permute-start | bytes 12582920 | tf_op jit(solution)/shard_map/ppermute | solution.py:151
  285.2 4.0 copy-start.26
  285.2 4.1 copy-start.23
  286.8 48.7 %collective-permute-start.1 = (bf16[128,8192]{1,0:T(8,128)(2,1)}, bf16[128,8192]{1,0:T(8,128)(2,1)}, u32[]{:S(2)}, u32[]{:S(2)}) collective-permute-start(bf16[128,8192]{1,0:T(8,128)(2,1)} %fusion.26), channel_id=1, source_target_pairs={{0,2},{1,3},{2,0},{3,1},{4,6},{5,7},{6,4},{7,5},{8,10},{9,11},{10,... | collective-permute-start | bytes 6291464 | tf_op jit(solution)/shard_map/ppermute | solution.py:156
  289.3 46.2 %copy-start.1 = (f32[2,128,8192]{2,1,0:T(8,128)S(1)}, f32[2,128,8192]{2,1,0:T(8,128)}, u32[]{:S(2)}) copy-start(f32[2,128,8192]{2,1,0:T(8,128)} %copy-done) | copy-start | bytes 25165828
  289.3 46.2 %copy-start.2 = (bf16[1,128,8192]{2,1,0:T(8,128)(2,1)S(1)}, bf16[1,128,8192]{2,1,0:T(8,128)(2,1)}, u32[]{:S(2)}) copy-start(bf16[1,128,8192]{2,1,0:T(8,128)(2,1)} %param.19) | copy-start | bytes 6291460
  335.5 13.1 %slice-start.11 = ((s8[8650752]{0:T(1024)(128)(4,1)}), s8[4194304]{0:T(1024)(128)(4,1)S(1)}, s32[]{:S(2)}) async-start(s8[8650752]{0:T(1024)(128)(4,1)} %bitcast.225), calls=%async_computation.20 | async-start | bytes 8388608
  335.5 13.1 %slice-start.12 = ((s8[8650752]{0:T(1024)(128)(4,1)}), s8[4194304]{0:T(1024)(128)(4,1)S(1)}, s32[]{:S(2)}) async-start(s8[8650752]{0:T(1024)(128)(4,1)} %bitcast.225), calls=%async_computation.21 | async-start | bytes 8388608
  338.6 10.1 %slice-start.13 = ((s8[8650752]{0:T(1024)(128)(4,1)}), s8[262144]{0:T(1024)(128)(4,1)S(1)}, s32[]{:S(2)}) async-start(s8[8650752]{0:T(1024)(128)(4,1)} %bitcast.225), calls=%async_computation.22 | async-start | bytes 524288
  343.2 7.7 %copy-start.7 = (bf16[4224,128]{0,1:T(8,128)(2,1)S(1)}, bf16[4224,128]{0,1:T(8,128)(2,1)}, u32[]{:S(2)}) copy-start(bf16[4224,128]{0,1:T(8,128)(2,1)} %fusion.19) | copy-start | bytes 3244036
  343.2 8.5 %copy-start.9 = (bf16[512,512]{0,1:T(8,128)(2,1)S(1)}, bf16[512,512]{0,1:T(8,128)(2,1)}, u32[]{:S(2)}) copy-start(bf16[512,512]{0,1:T(8,128)(2,1)} %copy-done.8) | copy-start | bytes 1572868
  343.2 26.3 %collective-permute-start.4 = (bf16[128,8192]{1,0:T(8,128)(2,1)}, bf16[128,8192]{1,0:T(8,128)(2,1)}, u32[]{:S(2)}, u32[]{:S(2)}) collective-permute-start(bf16[128,8192]{1,0:T(8,128)(2,1)} %fusion.58), channel_id=1, source_target_pairs={{96,0},{97,1},{98,2},{99,3},{100,4},{101,5},{102,6},{103,7},{104,8... | collective-permute-start | bytes 6291464 | tf_op jit(solution)/shard_map/ppermute | solution.py:169
  345.4 49.7 %collective-permute-start.3 = (bf16[128,8192]{1,0:T(8,128)(2,1)}, bf16[128,8192]{1,0:T(8,128)(2,1)}, u32[]{:S(2)}, u32[]{:S(2)}) collective-permute-start(bf16[128,8192]{1,0:T(8,128)(2,1)} %fusion.58), channel_id=1, source_target_pairs={{64,0},{96,32},{65,1},{97,33},{66,2},{98,34},{67,3},{99,35},{68,4}... | collective-permute-start | bytes 6291464 | tf_op jit(solution)/shard_map/ppermute | solution.py:169
  346.7 94.9 %collective-permute-start.2 = (bf16[128,8192]{1,0:T(8,128)(2,1)}, bf16[128,8192]{1,0:T(8,128)(2,1)}, u32[]{:S(2)}, u32[]{:S(2)}) collective-permute-start(bf16[128,8192]{1,0:T(8,128)(2,1)} %fusion.58), channel_id=1, source_target_pairs={{32,0},{64,32},{96,64},{33,1},{65,33},{97,65},{34,2},{66,34},{98,6... | collective-permute-start | bytes 6291464 | tf_op jit(solution)/shard_map/ppermute | solution.py:169
  352.6 14.8 %all-to-all-start.4 = ((bf16[4,128,512]{1,2,0:T(8,128)(2,1)}), bf16[4,128,512]{1,2,0:T(8,128)(2,1)S(1)}, u32[]{:S(2)}, u32[]{:S(2)}) async-start(bf16[4,128,512]{1,2,0:T(8,128)(2,1)} %copy_bitcast_fusion), calls=%async_computation.6 | async-start | bytes 1048576 | tf_op jit(solution)/shard_map/all_to_all | solution.py:130
  (10 other events, 20.9 us)
Sparse Core Ops, SparseCore 0:
  145.0 52.8 reduce-scatter.2
  200.2 51.8 reduce-scatter.4
